TPU v7x, 256 devices: a whole 4x4x8 slice. The times are simulated.
256 devices in a mesh: gx: 32 (over z_lo, y, core), gy: 4 (over x), gz: 2 (over z_hi).
Axes of the slice: x: 4, y: 4, z: 8 (z_hi: 2, z_lo: 4; z = z_hi * 4 + z_lo), core: 2. Of those that a mesh axis runs over, the one named last changes fastest.
Arguments:
- f_pop: float32 [19, 128, 64, 256], P(None, 'gx', 'gy', 'gz'), may hold values from 0.02 to 0.1
- g_pop: float32 [19, 128, 64, 256], P(None, 'gx', 'gy', 'gz'), may hold values from -0.2 to 0.2
- displacement: int32 [1], replicated, may hold values from 33 to 47
Outputs:
- f_new: float32 [19, 128, 64, 256], P(None, 'gx', 'gy', 'gz')
- g_new: float32 [19, 128, 64, 256], P(None, 'gx', 'gy', 'gz')
All inputs are finite; a program needn't handle non-finite values.
Results may differ from a plain program's by a relative error of at most 0.0001.
Values sent between devices are 32-bit elements; how exact they have to be, the bound alone decides.
No kernel may reach another device: no remote copies, remote signals or barrier semaphores. Data moves between devices by JAX's collectives and lax.ppermute only.
A program may use at most 64 MiB of HBM per device.

v0:
```python
import jax
import jax.numpy as jnp
from jax import lax
from jax.sharding import PartitionSpec as P

VELOCITIES = [
    (0, 0, 0),
    (1, 0, 0),
    (1, 1, 0),
    (1, -1, 0),
    (1, 0, 1),
    (1, 0, -1),
    (-1, 0, 0),
    (-1, -1, 0),
    (-1, 1, 0),
    (-1, 0, -1),
    (-1, 0, 1),
    (0, 1, 0),
    (0, -1, 0),
    (0, 0, 1),
    (0, 0, -1),
    (0, 1, 1),
    (0, -1, -1),
    (0, 1, -1),
    (0, -1, 1),
]
BULK_COEF = 0.5
STIFFNESS = 0.5
TAU_FLUID = 0.8
TAU_ORDER = 0.9


def with_halo(cells, sides, width):
    for axis, dim in sides:
        count = lax.axis_size(axis)
        head = lax.slice_in_dim(cells, 0, width, axis=dim)
        tail = lax.slice_in_dim(cells, cells.shape[dim] - width, cells.shape[dim], axis=dim)
        cells = jnp.concatenate(
            [
                lax.ppermute(tail, axis, [(i, (i + 1) % count) for i in range(count)]),
                cells,
                lax.ppermute(head, axis, [((i + 1) % count, i) for i in range(count)]),
            ],
            axis=dim,
        )
    return cells


def lattice_weight(number):
    steps_sq = sum((abs(comp) for comp in VELOCITIES[number]))
    if steps_sq == 0:
        return 1.0 / 3.0
    if steps_sq == 1:
        return 1.0 / 18.0
    return 1.0 / 36.0


def along(number, values, base):
    result = jnp.zeros_like(base)
    for axis_id in range(3):
        comp = VELOCITIES[number][axis_id]
        if comp != 0:
            result = result + comp * values[axis_id]
    return result


def collide(f_pop, g_pop, order_field, laplace, slopes):
    density = jnp.sum(f_pop, axis=0)
    chemical = (
        BULK_COEF * (order_field * order_field * order_field - order_field) - STIFFNESS * laplace
    )
    forces = [chemical * slope for slope in slopes]
    moments = []
    for axis_id in range(3):
        moment = jnp.zeros_like(density)
        for number in range(19):
            comp = VELOCITIES[number][axis_id]
            if comp != 0:
                moment = moment + comp * f_pop[number]
        moments.append(moment)
    flows = [(moments[axis_id] + 0.5 * forces[axis_id]) / density for axis_id in range(3)]
    speed_sq = flows[0] * flows[0] + flows[1] * flows[1] + flows[2] * flows[2]
    flow_force = flows[0] * forces[0] + flows[1] * forces[1] + flows[2] * forces[2]
    f_posts = []
    g_eqs = []
    for number in range(19):
        weight = lattice_weight(number)
        proj_flow = along(number, flows, density)
        proj_force = along(number, forces, density)
        shape_term = 3.0 * proj_flow + 4.5 * proj_flow * proj_flow - 1.5 * speed_sq
        f_eq = weight * density * (1.0 + shape_term)
        source = (
            (1.0 - 0.5 / TAU_FLUID)
            * weight
            * (3.0 * (proj_force - flow_force) + 9.0 * proj_flow * proj_force)
        )
        f_posts.append(f_pop[number] - (f_pop[number] - f_eq) / TAU_FLUID + source)
        g_eqs.append(weight * (3.0 * chemical + order_field * shape_term))
    rest_eq = order_field
    for number in range(1, 19):
        rest_eq = rest_eq - g_eqs[number]
    g_eqs[0] = rest_eq
    g_posts = [g_pop[number] - (g_pop[number] - g_eqs[number]) / TAU_ORDER for number in range(19)]
    return (jnp.stack(f_posts), jnp.stack(g_posts))


def window(whole, begin, rows, whole_rows):
    begin = jnp.mod(begin, whole_rows)
    doubled = jnp.concatenate([whole, whole], axis=1)
    return lax.dynamic_slice_in_dim(doubled, begin, rows, 1)


def sliding(edges, shift):
    extended = with_halo(edges, (("gx", 1),), 1)
    below = extended[:, 0]
    above = extended[:, 3]
    whole_below, whole_above = (
        lax.all_gather(below, "gy", axis=1, tiled=True),
        lax.all_gather(above, "gy", axis=1, tiled=True),
    )
    rows = below.shape[1]
    whole_rows = whole_below.shape[1]
    start = lax.axis_index("gy") * rows
    return (
        window(whole_below, start - shift, rows, whole_rows),
        window(whole_above, start + shift, rows, whole_rows),
    )


def extend_x(posts, below, above):
    rows, layers = (posts.shape[2], posts.shape[3])
    lower = jnp.concatenate(
        [
            jnp.zeros((1, rows, layers), jnp.float32),
            below,
            jnp.zeros((13, rows, layers), jnp.float32),
        ],
        axis=0,
    )
    upper = jnp.concatenate(
        [
            jnp.zeros((6, rows, layers), jnp.float32),
            above,
            jnp.zeros((8, rows, layers), jnp.float32),
        ],
        axis=0,
    )
    return jnp.concatenate([lower[:, None], posts, upper[:, None]], axis=1)


def local(f_pop, g_pop, displacement):
    shift = displacement[0]
    width_x, width_y, width_z = (f_pop.shape[1], f_pop.shape[2], f_pop.shape[3])
    order_field = jnp.sum(g_pop, axis=0)
    phase_edges = jnp.stack([order_field[0], order_field[-1]])[None]
    phase_below, phase_above = sliding(phase_edges, shift)
    neigh_xm = jnp.concatenate([phase_below, order_field[:-1]], axis=0)
    neigh_xp = jnp.concatenate([order_field[1:], phase_above], axis=0)
    padded = with_halo(order_field, (("gy", 1), ("gz", 2)), 1)
    neigh_ym = padded[:, :-2, 1:-1]
    neigh_yp = padded[:, 2:, 1:-1]
    neigh_zm = padded[:, 1:-1, :-2]
    neigh_zp = padded[:, 1:-1, 2:]
    laplace = neigh_xm + neigh_xp + neigh_ym + neigh_yp + neigh_zm + neigh_zp - 6.0 * order_field
    slopes = [0.5 * (neigh_xp - neigh_xm), 0.5 * (neigh_yp - neigh_ym), 0.5 * (neigh_zp - neigh_zm)]
    f_post, g_post = collide(f_pop, g_pop, order_field, laplace, slopes)
    pop_edges = jnp.concatenate(
        [
            jnp.stack([f_post[6:11, 0], f_post[1:6, -1]], axis=1),
            jnp.stack([g_post[6:11, 0], g_post[1:6, -1]], axis=1),
        ],
        axis=0,
    )
    pop_below, pop_above = sliding(pop_edges, shift)
    layered = jnp.concatenate(
        [
            extend_x(f_post, pop_below[0:5], pop_above[0:5]),
            extend_x(g_post, pop_below[5:10], pop_above[5:10]),
        ],
        axis=0,
    )
    results = []
    padded_all = with_halo(layered, (("gy", 2), ("gz", 3)), 1)
    for number in range(38):
        vel_x, vel_y, vel_z = VELOCITIES[number % 19]
        results.append(
            padded_all[
                number,
                1 - vel_x : 1 - vel_x + width_x,
                1 - vel_y : 1 - vel_y + width_y,
                1 - vel_z : 1 - vel_z + width_z,
            ]
        )
    f_new = jnp.stack(results[:19])
    g_new = jnp.stack(results[19:])
    return (f_new, g_new)


def solution(mesh):
    return jax.shard_map(
        local,
        mesh=mesh,
        in_specs=(P(None, "gx", "gy", "gz"), P(None, "gx", "gy", "gz"), P()),
        out_specs=(P(None, "gx", "gy", "gz"), P(None, "gx", "gy", "gz")),
        check_vma=False,
    )
```

profile of v0, /device:TPU:6, one launch (start us, length us, event | category | flops | bytes accessed | tf_op | source)
XLA Modules:
  0.0 120.2 jit_solution(16818710644719364818)
XLA Ops:
  0.7 1.2 %reduce_sum.19 = f32[4,16,128]{2,1,0:T(8,128)S(1)} reduce(f32[19,4,16,128]{3,2,1,0:T(8,128)} %param.4, f32[]{:T(128)} %constant.95.clone.1), dimensions={0}, to_apply=%region_1.2 | reduce | flops 147456 | bytes 655364 | tf_op jit(solution)/shard_map/reduce_sum | solution.py:154
  1.9 0.9 collective-permute-start.3
  2.8 2.4 %collective-permute-start.2 = (f32[4,1,128]{2,1,0:T(1,128)S(1)}, f32[4,1,128]{2,1,0:T(1,128)S(1)}, u32[]{:S(2)}, u32[]{:S(2)}) collective-permute-start(f32[4,1,128]{2,1,0:T(1,128)S(1)} %get-tuple-element.109), channel_id=1, source_target_pairs={{0,2},{2,4},{4,6},{6,0},{1,3},{3,5},{5,7},{7,1},{8,10},{10,12},{12... | collective-permute-start | bytes 6152 | tf_op jit(solution)/shard_map/ppermute | solution.py:40
  5.2 6.0 %collective-permute-start.1 = (f32[1,1,16,128]{3,2,1,0:T(8,128)S(1)}, f32[1,1,16,128]{3,2,1,0:T(8,128)S(1)}, u32[]{:S(2)}, u32[]{:S(2)}) collective-permute-start(f32[1,1,16,128]{3,2,1,0:T(8,128)S(1)} %get-tuple-element.114), channel_id=1, source_target_pairs={{8,0},{16,8},{24,16},{32,24},{40,32},{48,40},{56,48},{64,56},{72,6... | collective-permute-start | bytes 24584 | tf_op jit(solution)/shard_map/ppermute | solution.py:42
  12.0 0.1 pad.67.clone
  12.1 0.1 pad.60.clone
  12.1 1.1 reduce_sum.18
  13.3 0.1 fusion.109
  13.4 4.5 %collective-permute-start.5 = (f32[4,18,1]{2,1,0:T(8,128)S(1)}, f32[4,18,1]{2,1,0:T(8,128)S(1)}, u32[]{:S(2)}, u32[]{:S(2)}) collective-permute-start(f32[4,18,1]{2,1,0:T(8,128)S(1)} %get-tuple-element.106), channel_id=1, source_target_pairs={{1,0},{0,1},{3,2},{2,3},{5,4},{4,5},{7,6},{6,7},{9,8},{8,9},{11,10... | collective-permute-start | bytes 872 | tf_op jit(solution)/shard_map/ppermute | solution.py:42
  17.9 1.4 %collective-permute-start.4 = (f32[4,18,1]{2,1,0:T(8,128)S(1)}, f32[4,18,1]{2,1,0:T(8,128)S(1)}, u32[]{:S(2)}, u32[]{:S(2)}) collective-permute-start(f32[4,18,1]{2,1,0:T(8,128)S(1)} %get-tuple-element.107), channel_id=1, source_target_pairs={{0,1},{1,0},{2,3},{3,2},{4,5},{5,4},{6,7},{7,6},{8,9},{9,8},{10,11... | collective-permute-start | bytes 872 | tf_op jit(solution)/shard_map/ppermute | solution.py:40
  19.4 11.9 %all-gather = f32[1,1,64,128]{3,2,1,0:T(8,128)S(1)} all-gather(f32[1,1,16,128]{3,2,1,0:T(8,128)S(1)} %collective-permute-done), channel_id=2, replica_groups=mesh['gx'=32,'gy'=4,'gz'=2] {'gy'}, dimensions={2}, use_global_device_ids=true | all-gather | bytes 40960 | tf_op jit(solution)/shard_map/all_gather | solution.py:118
  31.3 11.9 %all-gather.1 = f32[1,1,64,128]{3,2,1,0:T(8,128)S(1)} all-gather(f32[1,1,16,128]{3,2,1,0:T(8,128)S(1)} %collective-permute-done.1), channel_id=3, replica_groups=mesh['gx'=32,'gy'=4,'gz'=2] {'gy'}, dimensions={2}, use_global_device_ids=true | all-gather | bytes 40960 | tf_op jit(solution)/shard_map/all_gather | solution.py:119
  43.2 1.4 %bitcast_subtract_fusion.16 = (f32[4,16,128]{2,1,0:T(8,128)S(1)}, f32[4,16,128]{2,1,0:T(8,128)S(1)}, f32[4,16,128]{2,1,0:T(8,128)S(1)}, f32[4,16,128]{2,1,0:T(8,...) fusion(f32[4,16,128]{2,1,0:T(8,128)S(1)} %reduce_sum.19, ...), kind=kLoop, calls=%fused_computation.190 | loop fusion | flops 2064384 | bytes 1512000 | tf_op jit(solution)/shard_map/sub | solution.py:103
  45.4 0.1 collective-permute-start.7
  45.5 0.5 collective-permute-start.6
  46.0 0.8 copy.371
  47.3 6.0 %collective-permute-done.6 = f32[10,1,16,128]{3,2,1,0:T(8,128)S(1)} collective-permute-done((f32[10,1,16,128]{3,2,1,0:T(8,128)S(1)}, f32[10,1,16,128]{3,2,1,0:T(8,128)S(1)}, u32[]{:S(2)}, u32[]{:S(2)}) %collective-permute-start.6) | collective-permute-done | bytes 81952 | tf_op jit(solution)/shard_map/ppermute | solution.py:40
  53.3 0.1 copy.282
  53.4 12.4 %all-gather.2 = f32[10,1,64,128]{3,1,0,2:T(1,128)S(1)} all-gather(f32[10,1,16,128]{3,1,0,2:T(1,128)S(1)} %copy.282), channel_id=4, replica_groups=mesh['gx'=32,'gy'=4,'gz'=2] {'gy'}, dimensions={2}, use_global_device_ids=true | all-gather | bytes 409600 | tf_op jit(solution)/shard_map/all_gather | solution.py:118
  65.9 0.1 copy.284
  66.0 12.4 %all-gather.3 = f32[10,1,64,128]{3,1,0,2:T(1,128)S(1)} all-gather(f32[10,1,16,128]{3,1,0,2:T(1,128)S(1)} %copy.284), channel_id=5, replica_groups=mesh['gx'=32,'gy'=4,'gz'=2] {'gy'}, dimensions={2}, use_global_device_ids=true | all-gather | bytes 409600 | tf_op jit(solution)/shard_map/all_gather | solution.py:119
  78.5 0.1 maximum_bitcast_fusion.2
  78.6 0.1 maximum_bitcast_fusion.1
  78.7 0.2 fusion
  78.9 0.7 collective-permute-start.8
  79.6 1.7 %collective-permute-start.9 = (f32[38,6,1,128]{3,0,2,1:T(8,128)S(1)}, f32[38,6,1,128]{3,0,2,1:T(8,128)S(1)}, u32[]{:S(2)}, u32[]{:S(2)}) collective-permute-start(f32[38,6,1,128]{3,0,2,1:T(8,128)S(1)} %copy.290), channel_id=1, source_target_pairs={{2,0},{4,2},{6,4},{0,6},{3,1},{5,3},{7,5},{1,7},{10,8},{12,10},{14... | collective-permute-start | bytes 350216 | tf_op jit(solution)/shard_map/ppermute | solution.py:42
  81.3 2.6 %collective-permute-done.8 = f32[38,6,1,128]{3,0,2,1:T(8,128)S(1)} collective-permute-done((f32[38,6,1,128]{3,0,2,1:T(8,128)S(1)}, f32[38,6,1,128]{3,0,2,1:T(8,128)S(1)}, u32[]{:S(2)}, u32[]{:S(2)}) %collective-permute-start.8) | collective-permute-done | bytes 116768 | tf_op jit(solution)/shard_map/ppermute | solution.py:40
  83.8 0.1 copy.289
  84.0 1.9 %collective-permute-done.9 = f32[38,6,1,128]{3,0,2,1:T(8,128)S(1)} collective-permute-done((f32[38,6,1,128]{3,0,2,1:T(8,128)S(1)}, f32[38,6,1,128]{3,0,2,1:T(8,128)S(1)}, u32[]{:S(2)}, u32[]{:S(2)}) %collective-permute-start.9) | collective-permute-done | bytes 116768 | tf_op jit(solution)/shard_map/ppermute | solution.py:42
  85.9 0.1 copy.291
  86.0 0.5 pad_maximum_fusion
  86.5 3.2 %fusion.105 = (f32[38,6,18,1]{3,2,1,0:T(8,128)}, f32[38,6,18,1]{3,2,1,0:T(8,128)}) fusion(f32[38,6,18,128]{3,2,1,0:T(8,128)S(1)} %pad_maximum_fusion), kind=kLoop, calls=%fused_computation.399 | loop fusion | bytes 65664 | tf_op jit(solution)/shard_map/slice | solution.py:36
  89.7 3.0 %copy.294 = f32[38,6,18,1]{0,2,3,1:T(8,128)S(1)} copy(f32[38,6,18,1]{3,2,1,0:T(8,128)} %get-tuple-element.53) | data formatting | bytes 32832 | tf_op jit(solution)/shard_map/slice | solution.py:37
  92.8 4.6 %collective-permute-start.10 = (f32[38,6,18,1]{0,2,3,1:T(8,128)S(1)}, f32[38,6,18,1]{0,2,3,1:T(8,128)S(1)}, u32[]{:S(2)}, u32[]{:S(2)}) collective-permute-start(f32[38,6,18,1]{0,2,3,1:T(8,128)S(1)} %copy.294), channel_id=1, source_target_pairs={{0,1},{1,0},{2,3},{3,2},{4,5},{5,4},{6,7},{7,6},{8,9},{9,8},{10,11... | collective-permute-start | bytes 49256 | tf_op jit(solution)/shard_map/ppermute | solution.py:40
  97.4 3.0 %copy.296 = f32[38,6,18,1]{0,2,3,1:T(8,128)S(1)} copy(f32[38,6,18,1]{3,2,1,0:T(8,128)} %get-tuple-element.52) | data formatting | bytes 32832 | tf_op jit(solution)/shard_map/slice | solution.py:36
  100.4 1.5 %collective-permute-start.11 = (f32[38,6,18,1]{0,2,3,1:T(8,128)S(1)}, f32[38,6,18,1]{0,2,3,1:T(8,128)S(1)}, u32[]{:S(2)}, u32[]{:S(2)}) collective-permute-start(f32[38,6,18,1]{0,2,3,1:T(8,128)S(1)} %copy.296), channel_id=1, source_target_pairs={{1,0},{0,1},{3,2},{2,3},{5,4},{4,5},{7,6},{6,7},{9,8},{8,9},{11,10... | collective-permute-start | bytes 49256 | tf_op jit(solution)/shard_map/ppermute | solution.py:42
  101.9 2.8 %copy.295 = f32[38,6,18,1]{3,2,1,0:T(8,128)} copy(f32[38,6,18,1]{0,2,3,1:T(8,128)S(1)} %collective-permute-done.10) | data formatting | bytes 32832 | tf_op jit(solution)/shard_map/ppermute | solution.py:40
  104.7 0.9 constant_dynamic-update-slice_fusion.91
  105.5 3.2 %collective-permute-done.11 = f32[38,6,18,1]{0,2,3,1:T(8,128)S(1)} collective-permute-done((f32[38,6,18,1]{0,2,3,1:T(8,128)S(1)}, f32[38,6,18,1]{0,2,3,1:T(8,128)S(1)}, u32[]{:S(2)}, u32[]{:S(2)}) %collective-permute-start.11) | collective-permute-done | bytes 16448 | tf_op jit(solution)/shard_map/ppermute | solution.py:42
  108.7 2.8 %copy.297 = f32[38,6,18,1]{3,2,1,0:T(8,128)} copy(f32[38,6,18,1]{0,2,3,1:T(8,128)S(1)} %collective-permute-done.11) | data formatting | bytes 32832 | tf_op jit(solution)/shard_map/ppermute | solution.py:42
  111.5 0.9 constant_dynamic-update-slice_fusion.90
  112.5 1.7 %copy-done.1 = f32[38,6,18,1]{3,2,1,0:T(8,128)S(1)} copy-done((f32[38,6,18,1]{3,2,1,0:T(8,128)S(1)}, f32[38,6,18,1]{3,2,1,0:T(8,128)}, u32[]{:S(2)}) %copy-start.1) | copy-done | bytes 16440
  114.2 0.1 constant_dynamic-update-slice_fusion.86
  114.3 1.7 %copy-done = f32[38,6,18,1]{3,2,1,0:T(8,128)S(1)} copy-done((f32[38,6,18,1]{3,2,1,0:T(8,128)S(1)}, f32[38,6,18,1]{3,2,1,0:T(8,128)}, u32[]{:S(2)}) %copy-start) | copy-done | bytes 16440
  116.0 0.1 constant_dynamic-update-slice_fusion.85
  116.1 0.1 constant_dynamic-update-slice_fusion.82
  116.2 0.1 constant_dynamic-update-slice_fusion.81
  116.3 1.0 copy-done.5
  117.3 0.1 constant_dynamic-update-slice_fusion.80
  117.4 0.1 constant_dynamic-update-slice_fusion.79
  117.5 0.1 constant_dynamic-update-slice_fusion.72
  117.6 0.1 constant_dynamic-update-slice_fusion.71
  117.7 0.1 constant_dynamic-update-slice_fusion.78
  117.8 0.1 constant_dynamic-update-slice_fusion.67
  117.9 0.1 constant_dynamic-update-slice_fusion.66
  118.0 0.1 constant_dynamic-update-slice_fusion.77
  118.1 0.1 constant_dynamic-update-slice_fusion.63
  118.2 0.7 copy-done.4
  118.9 0.1 constant_dynamic-update-slice_fusion.62
  119.0 0.1 constant_dynamic-update-slice_fusion.61
  119.1 0.1 constant_dynamic-update-slice_fusion.60
  119.2 0.1 constant_dynamic-update-slice_fusion.59
  119.3 0.1 constant_dynamic-update-slice_fusion.58
  119.4 0.8 copy-done.6
  (97 shorter events, 1.3 us)
Async XLA Ops:
  0.6 44.2 %copy-start.3 = (f32[19,4,16,128]{3,2,1,0:T(8,128)S(1)}, f32[19,4,16,128]{3,2,1,0:T(8,128)}, u32[]{:S(2)}) copy-start(f32[19,4,16,128]{3,2,1,0:T(8,128)} %param.4) | copy-start | bytes 1867780
  0.6 44.0 %copy-start.2 = (f32[19,4,16,128]{3,2,1,0:T(8,128)S(1)}, f32[19,4,16,128]{3,2,1,0:T(8,128)}, u32[]{:S(2)}) copy-start(f32[19,4,16,128]{3,2,1,0:T(8,128)} %param.3) | copy-start | bytes 1867780
  1.9 11.4 %collective-permute-start.3 = (f32[4,1,128]{2,1,0:T(1,128)S(1)}, f32[4,1,128]{2,1,0:T(1,128)S(1)}, u32[]{:S(2)}, u32[]{:S(2)}) collective-permute-start(f32[4,1,128]{2,1,0:T(1,128)S(1)} %get-tuple-element.108), channel_id=1, source_target_pairs={{2,0},{4,2},{6,4},{0,6},{3,1},{5,3},{7,5},{1,7},{10,8},{12,10},{14... | collective-permute-start | bytes 6152 | tf_op jit(solution)/shard_map/ppermute | solution.py:42
  2.8 10.5 %collective-permute-start.2 = (f32[4,1,128]{2,1,0:T(1,128)S(1)}, f32[4,1,128]{2,1,0:T(1,128)S(1)}, u32[]{:S(2)}, u32[]{:S(2)}) collective-permute-start(f32[4,1,128]{2,1,0:T(1,128)S(1)} %get-tuple-element.109), channel_id=1, source_target_pairs={{0,2},{2,4},{4,6},{6,0},{1,3},{3,5},{5,7},{7,1},{8,10},{10,12},{12... | collective-permute-start | bytes 6152 | tf_op jit(solution)/shard_map/ppermute | solution.py:40
  5.2 26.1 %collective-permute-start.1 = (f32[1,1,16,128]{3,2,1,0:T(8,128)S(1)}, f32[1,1,16,128]{3,2,1,0:T(8,128)S(1)}, u32[]{:S(2)}, u32[]{:S(2)}) collective-permute-start(f32[1,1,16,128]{3,2,1,0:T(8,128)S(1)} %get-tuple-element.114), channel_id=1, source_target_pairs={{8,0},{16,8},{24,16},{32,24},{40,32},{48,40},{56,48},{64,56},{72,6... | collective-permute-start | bytes 24584 | tf_op jit(solution)/shard_map/ppermute | solution.py:42
  11.2 8.1 %collective-permute-start = (f32[1,1,16,128]{3,2,1,0:T(8,128)S(1)}, f32[1,1,16,128]{3,2,1,0:T(8,128)S(1)}, u32[]{:S(2)}, u32[]{:S(2)}) collective-permute-start(f32[1,1,16,128]{3,2,1,0:T(8,128)S(1)} %get-tuple-element.115), channel_id=1, source_target_pairs={{0,8},{8,16},{16,24},{24,32},{32,40},{40,48},{48,56},{56,64},{64,7... | collective-permute-start | bytes 24584 | tf_op jit(solution)/shard_map/ppermute | solution.py:40
  13.4 29.9 %collective-permute-start.5 = (f32[4,18,1]{2,1,0:T(8,128)S(1)}, f32[4,18,1]{2,1,0:T(8,128)S(1)}, u32[]{:S(2)}, u32[]{:S(2)}) collective-permute-start(f32[4,18,1]{2,1,0:T(8,128)S(1)} %get-tuple-element.106), channel_id=1, source_target_pairs={{1,0},{0,1},{3,2},{2,3},{5,4},{4,5},{7,6},{6,7},{9,8},{8,9},{11,10... | collective-permute-start | bytes 872 | tf_op jit(solution)/shard_map/ppermute | solution.py:42
  17.9 25.3 %collective-permute-start.4 = (f32[4,18,1]{2,1,0:T(8,128)S(1)}, f32[4,18,1]{2,1,0:T(8,128)S(1)}, u32[]{:S(2)}, u32[]{:S(2)}) collective-permute-start(f32[4,18,1]{2,1,0:T(8,128)S(1)} %get-tuple-element.107), channel_id=1, source_target_pairs={{0,1},{1,0},{2,3},{3,2},{4,5},{5,4},{6,7},{7,6},{8,9},{9,8},{10,11... | collective-permute-start | bytes 872 | tf_op jit(solution)/shard_map/ppermute | solution.py:40
  45.4 20.5 %collective-permute-start.7 = (f32[10,1,16,128]{3,2,1,0:T(8,128)S(1)}, f32[10,1,16,128]{3,2,1,0:T(8,128)S(1)}, u32[]{:S(2)}, u32[]{:S(2)}) collective-permute-start(f32[10,1,16,128]{3,2,1,0:T(8,128)S(1)} %get-tuple-element.92), channel_id=1, source_target_pairs={{8,0},{16,8},{24,16},{32,24},{40,32},{48,40},{56,48},{64,56},{72,6... | collective-permute-start | bytes 245768 | tf_op jit(solution)/shard_map/ppermute | solution.py:42
  45.5 7.9 %collective-permute-start.6 = (f32[10,1,16,128]{3,2,1,0:T(8,128)S(1)}, f32[10,1,16,128]{3,2,1,0:T(8,128)S(1)}, u32[]{:S(2)}, u32[]{:S(2)}) collective-permute-start(f32[10,1,16,128]{3,2,1,0:T(8,128)S(1)} %get-tuple-element.93), channel_id=1, source_target_pairs={{0,8},{8,16},{16,24},{24,32},{32,40},{40,48},{48,56},{56,64},{64,7... | collective-permute-start | bytes 245768 | tf_op jit(solution)/shard_map/ppermute | solution.py:40
  78.9 5.0 %collective-permute-start.8 = (f32[38,6,1,128]{3,0,2,1:T(8,128)S(1)}, f32[38,6,1,128]{3,0,2,1:T(8,128)S(1)}, u32[]{:S(2)}, u32[]{:S(2)}) collective-permute-start(f32[38,6,1,128]{3,0,2,1:T(8,128)S(1)} %copy.288), channel_id=1, source_target_pairs={{0,2},{2,4},{4,6},{6,0},{1,3},{3,5},{5,7},{7,1},{8,10},{10,12},{12... | collective-permute-start | bytes 350216 | tf_op jit(solution)/shard_map/ppermute | solution.py:40
  79.6 6.3 %collective-permute-start.9 = (f32[38,6,1,128]{3,0,2,1:T(8,128)S(1)}, f32[38,6,1,128]{3,0,2,1:T(8,128)S(1)}, u32[]{:S(2)}, u32[]{:S(2)}) collective-permute-start(f32[38,6,1,128]{3,0,2,1:T(8,128)S(1)} %copy.290), channel_id=1, source_target_pairs={{2,0},{4,2},{6,4},{0,6},{3,1},{5,3},{7,5},{1,7},{10,8},{12,10},{14... | collective-permute-start | bytes 350216 | tf_op jit(solution)/shard_map/ppermute | solution.py:42
  92.8 9.1 %collective-permute-start.10 = (f32[38,6,18,1]{0,2,3,1:T(8,128)S(1)}, f32[38,6,18,1]{0,2,3,1:T(8,128)S(1)}, u32[]{:S(2)}, u32[]{:S(2)}) collective-permute-start(f32[38,6,18,1]{0,2,3,1:T(8,128)S(1)} %copy.294), channel_id=1, source_target_pairs={{0,1},{1,0},{2,3},{3,2},{4,5},{5,4},{6,7},{7,6},{8,9},{9,8},{10,11... | collective-permute-start | bytes 49256 | tf_op jit(solution)/shard_map/ppermute | solution.py:40
  100.4 8.3 %collective-permute-start.11 = (f32[38,6,18,1]{0,2,3,1:T(8,128)S(1)}, f32[38,6,18,1]{0,2,3,1:T(8,128)S(1)}, u32[]{:S(2)}, u32[]{:S(2)}) collective-permute-start(f32[38,6,18,1]{0,2,3,1:T(8,128)S(1)} %copy.296), channel_id=1, source_target_pairs={{1,0},{0,1},{3,2},{2,3},{5,4},{4,5},{7,6},{6,7},{9,8},{8,9},{11,10... | collective-permute-start | bytes 49256 | tf_op jit(solution)/shard_map/ppermute | solution.py:42
  112.4 1.8 %copy-start.1 = (f32[38,6,18,1]{3,2,1,0:T(8,128)S(1)}, f32[38,6,18,1]{3,2,1,0:T(8,128)}, u32[]{:S(2)}) copy-start(f32[38,6,18,1]{3,2,1,0:T(8,128)} %copy.297) | copy-start | bytes 49252
  114.2 1.8 %copy-start = (f32[38,6,18,1]{3,2,1,0:T(8,128)S(1)}, f32[38,6,18,1]{3,2,1,0:T(8,128)}, u32[]{:S(2)}) copy-start(f32[38,6,18,1]{3,2,1,0:T(8,128)} %copy.295) | copy-start | bytes 49252
  116.2 1.1 copy-start.5
  118.1 0.8 copy-start.4
  119.4 0.8 copy-start.6
where the time goes:
time: 121 us; the launch traced here: 120 us
  blocking collectives  48.6 us (40%)
  starting transfers between devices  24.3 us (20%)
  local copies, waits for them, and re-layouts  22.6 us (19%)
  waiting for transfers between devices  13.7 us (11%)
  other arithmetic  8.9 us (7%)
  between operations  2.11 us (2%)
    all_gather x2, blocking collectives, sliding(): lax.all_gather(above, 'gy', axis=1, tiled=True)  24.3 us
    all_gather x2, blocking collectives, sliding(): lax.all_gather(below, 'gy', axis=1, tiled=True)  24.3 us
    ppermute x6, starting transfers between devices, with_halo(): lax.ppermute(head, axis, [((i + 1) % count, i) for i in range(count)])  14.7 us
    ppermute x6, starting transfers between devices, with_halo(): lax.ppermute(tail, axis, [(i, (i + 1) % count) for i in range(count)])  9.57 us
    ppermute x6, waiting for transfers between devices, with_halo(): lax.ppermute(tail, axis, [(i, (i + 1) % count) for i in range(count)])  8.57 us
    unnamed x27, local copies, waits for them, and re-layouts  6.9 us
    slice x7, local copies, waits for them, and re-layouts, with_halo(): head = lax.slice_in_dim(cells, 0, width, axis=dim)  6.39 us
    ppermute x6, waiting for transfers between devices, with_halo(): lax.ppermute(head, axis, [((i + 1) % count, i) for i in range(count)])  5.11 us
  transfers between devices with their start and end apart: 12, of which 4 were waited for; matrix products, arithmetic and copies ran while one was open for 8% of the time, Pallas kernels for 0%

commit v1 on v0

--- a/solution.py
+++ b/solution.py
@@ -115,7 +115,9 @@
     below = extended[:, 0]
     above = extended[:, 3]
     whole_below, whole_above = (
-        lax.all_gather(below, "gy", axis=1, tiled=True),
+        jnp.concatenate(
+            lax.all_to_all(jnp.stack([below] * lax.axis_size("gy")), "gy", 0, 0), axis=1
+        ),
         lax.all_gather(above, "gy", axis=1, tiled=True),
     )
     rows = below.shape[1]

time: 121 us -> 110 us (0.909)
  blocking collectives: 48.6 us -> 24.3 us
  starting transfers between devices: 24.3 us -> 34.5 us
  waiting for transfers between devices: 13.7 us -> 15.4 us
    all_gather x2 -> x0, blocking collectives: 24.3 us -> none  [sliding(): lax.all_gather(below, 'gy', axis=1, tiled=True)]
    all_to_all x0 -> x2, starting transfers between devices: none -> 9.01 us  [sliding(): lax.all_to_all(jnp.stack([below] * lax.axis_size('gy')), 'gy', 0, 0)]
    another operation x3 -> x5, local copies, waits for them, and re-layouts: 0.01 us -> 1.37 us  [the longest x2 1.37 us: sliding(): jnp.stack([below] * lax.axis_size('gy'))]
    ppermute x6, waiting for transfers between devices: 5.11 us -> 6.43 us  [with_halo(): lax.ppermute(head, axis, [((i + 1) % count, i) for i in range(count)])]
    unnamed x27 -> x25, local copies, waits for them, and re-layouts: 6.9 us -> 7.14 us
    ppermute x3 -> x2, local copies, waits for them, and re-layouts: 2.97 us -> 2.8 us  [with_halo(): lax.ppermute(tail, axis, [(i, (i + 1) % count) for i in range(count)])]
    unnamed x56 -> x60, other arithmetic: 3.92 us -> 3.97 us
  transfers between devices with their start and end apart: 12 -> 14, of which waited for: 4 -> 4; matrix products, arithmetic and copies ran while one was open for 8% -> 10% of each run, Pallas kernels for 0% -> 0%
where the time goes in v1:
time: 110 us; the launch traced here: 109 us
  starting transfers between devices  34.5 us (31%)
  blocking collectives  24.3 us (22%)
  local copies, waits for them, and re-layouts  23.6 us (21%)
  waiting for transfers between devices  15.4 us (14%)
  other arithmetic  8.94 us (8%)
  between operations  2.11 us (2%)
    all_gather x2, blocking collectives, sliding(): lax.all_gather(above, 'gy', axis=1, tiled=True)  24.3 us
    ppermute x6, starting transfers between devices, with_halo(): lax.ppermute(head, axis, [((i + 1) % count, i) for i in range(count)])  15.1 us
    ppermute x6, starting transfers between devices, with_halo(): lax.ppermute(tail, axis, [(i, (i + 1) % count) for i in range(count)])  10.3 us
    all_to_all x2, starting transfers between devices, sliding(): lax.all_to_all(jnp.stack([below] * lax.axis_size('gy')), 'gy', 0, 0)  9.01 us
    ppermute x6, waiting for transfers between devices, with_halo(): lax.ppermute(tail, axis, [(i, (i + 1) % count) for i in range(count)])  8.96 us
    unnamed x25, local copies, waits for them, and re-layouts  7.14 us
    ppermute x6, waiting for transfers between devices, with_halo(): lax.ppermute(head, axis, [((i + 1) % count, i) for i in range(count)])  6.43 us
    slice x7, local copies, waits for them, and re-layouts, with_halo(): head = lax.slice_in_dim(cells, 0, width, axis=dim)  6.24 us
  transfers between devices with their start and end apart: 14, of which 4 were waited for; matrix products, arithmetic and copies ran while one was open for 10% of the time, Pallas kernels for 0%

profile of v1, /device:TPU:6, one launch (start us, length us, event | category | flops | bytes accessed | tf_op | source)
XLA Modules:
  0.0 108.9 jit_solution(635646805045040462)
XLA Ops:
  0.7 1.2 %reduce_sum.19 = f32[4,16,128]{2,1,0:T(8,128)S(1)} reduce(f32[19,4,16,128]{3,2,1,0:T(8,128)} %param.4, f32[]{:T(128)} %constant.95.clone.1), dimensions={0}, to_apply=%region_1.2 | reduce | flops 147456 | bytes 655364 | tf_op jit(solution)/shard_map/reduce_sum | solution.py:156
  1.9 0.9 collective-permute-start.3
  2.8 2.4 %collective-permute-start.2 = (f32[4,1,128]{2,1,0:T(1,128)S(1)}, f32[4,1,128]{2,1,0:T(1,128)S(1)}, u32[]{:S(2)}, u32[]{:S(2)}) collective-permute-start(f32[4,1,128]{2,1,0:T(1,128)S(1)} %get-tuple-element.101), channel_id=1, source_target_pairs={{0,2},{2,4},{4,6},{6,0},{1,3},{3,5},{5,7},{7,1},{8,10},{10,12},{12... | collective-permute-start | bytes 6152 | tf_op jit(solution)/shard_map/ppermute | solution.py:40
  5.2 6.0 %collective-permute-start.1 = (f32[1,1,16,128]{3,2,1,0:T(8,128)S(1)}, f32[1,1,16,128]{3,2,1,0:T(8,128)S(1)}, u32[]{:S(2)}, u32[]{:S(2)}) collective-permute-start(f32[1,1,16,128]{3,2,1,0:T(8,128)S(1)} %get-tuple-element.106), channel_id=1, source_target_pairs={{8,0},{16,8},{24,16},{32,24},{40,32},{48,40},{56,48},{64,56},{72,6... | collective-permute-start | bytes 24584 | tf_op jit(solution)/shard_map/ppermute | solution.py:42
  12.0 0.1 pad.67.clone
  12.1 0.1 pad.60.clone
  12.1 1.1 %reduce_sum.18 = f32[4,16,128]{2,1,0:T(8,128)S(1)} reduce(f32[19,4,16,128]{3,2,1,0:T(8,128)} %param.3, f32[]{:T(128)} %constant.95.clone.1), dimensions={0}, to_apply=%region_0.0 | reduce | flops 147456 | bytes 655364 | tf_op jit(solution)/shard_map/reduce_sum | solution.py:68
  13.3 0.1 fusion.109
  13.4 4.5 %collective-permute-start.5 = (f32[4,18,1]{2,1,0:T(8,128)S(1)}, f32[4,18,1]{2,1,0:T(8,128)S(1)}, u32[]{:S(2)}, u32[]{:S(2)}) collective-permute-start(f32[4,18,1]{2,1,0:T(8,128)S(1)} %get-tuple-element.98), channel_id=1, source_target_pairs={{1,0},{0,1},{3,2},{2,3},{5,4},{4,5},{7,6},{6,7},{9,8},{8,9},{11,10... | collective-permute-start | bytes 872 | tf_op jit(solution)/shard_map/ppermute | solution.py:42
  17.9 1.4 %collective-permute-start.4 = (f32[4,18,1]{2,1,0:T(8,128)S(1)}, f32[4,18,1]{2,1,0:T(8,128)S(1)}, u32[]{:S(2)}, u32[]{:S(2)}) collective-permute-start(f32[4,18,1]{2,1,0:T(8,128)S(1)} %get-tuple-element.99), channel_id=1, source_target_pairs={{0,1},{1,0},{2,3},{3,2},{4,5},{5,4},{6,7},{7,6},{8,9},{9,8},{10,11... | collective-permute-start | bytes 872 | tf_op jit(solution)/shard_map/ppermute | solution.py:40
  19.4 0.6 stack.152
  20.0 4.5 %all-to-all-start = ((f32[4,1,16,128]{3,2,1,0:T(8,128)}), f32[4,1,16,128]{3,2,1,0:T(8,128)S(1)}, u32[]{:S(2)}, u32[]{:S(2)}) async-start(f32[4,1,16,128]{3,2,1,0:T(8,128)} %stack.152), calls=%async_computation | async-start | bytes 65536 | tf_op jit(solution)/shard_map/all_to_all | solution.py:119
  24.5 11.9 %all-gather = f32[1,1,64,128]{3,2,1,0:T(8,128)S(1)} all-gather(f32[1,1,16,128]{3,2,1,0:T(8,128)S(1)} %collective-permute-done.1), channel_id=2, replica_groups=mesh['gx'=32,'gy'=4,'gz'=2] {'gy'}, dimensions={2}, use_global_device_ids=true | all-gather | bytes 40960 | tf_op jit(solution)/shard_map/all_gather | solution.py:121
  36.5 1.4 %bitcast_subtract_fusion.16 = (f32[4,16,128]{2,1,0:T(8,128)S(1)}, f32[4,16,128]{2,1,0:T(8,128)S(1)}, f32[4,16,128]{2,1,0:T(8,128)S(1)}, f32[4,16,128]{2,1,0:T(8,...) fusion(f32[4,16,128]{2,1,0:T(8,128)S(1)} %reduce_sum.19, ...), kind=kLoop, calls=%fused_computation.191 | loop fusion | flops 2064384 | bytes 1512000 | tf_op jit(solution)/shard_map/sub | solution.py:103
  38.6 1.7 %collective-permute-start.7 = (f32[10,1,16,128]{3,2,0,1:T(8,128)S(1)}, f32[10,1,16,128]{3,2,0,1:T(8,128)S(1)}, u32[]{:S(2)}, u32[]{:S(2)}) collective-permute-start(f32[10,1,16,128]{3,2,0,1:T(8,128)S(1)} %get-tuple-element.84), channel_id=1, source_target_pairs={{8,0},{16,8},{24,16},{32,24},{40,32},{48,40},{56,48},{64,56},{72,6... | collective-permute-start | bytes 245768 | tf_op jit(solution)/shard_map/ppermute | solution.py:42
  40.4 0.8 copy.352
  41.7 6.4 %collective-permute-done.6 = f32[10,1,16,128]{3,2,0,1:T(8,128)S(1)} collective-permute-done((f32[10,1,16,128]{3,2,0,1:T(8,128)S(1)}, f32[10,1,16,128]{3,2,0,1:T(8,128)S(1)}, u32[]{:S(2)}, u32[]{:S(2)}) %collective-permute-start.6) | collective-permute-done | bytes 81952 | tf_op jit(solution)/shard_map/ppermute | solution.py:40
  48.1 0.7 stack.180
  48.9 4.5 %all-to-all-start.1 = ((f32[4,10,16,128]{3,2,1,0:T(8,128)}), f32[4,10,16,128]{3,2,1,0:T(8,128)S(1)}, u32[]{:S(2)}, u32[]{:S(2)}) async-start(f32[4,10,16,128]{3,2,1,0:T(8,128)} %stack.180), calls=%async_computation.1 | async-start | bytes 655360 | tf_op jit(solution)/shard_map/all_to_all | solution.py:119
  53.4 0.1 copy.247
  53.5 12.4 %all-gather.1 = f32[10,1,64,128]{3,1,0,2:T(1,128)S(1)} all-gather(f32[10,1,16,128]{3,1,0,2:T(1,128)S(1)} %copy.247), channel_id=3, replica_groups=mesh['gx'=32,'gy'=4,'gz'=2] {'gy'}, dimensions={2}, use_global_device_ids=true | all-gather | bytes 409600 | tf_op jit(solution)/shard_map/all_gather | solution.py:121
  65.9 0.1 maximum_bitcast_fusion.1
  66.2 0.1 maximum_bitcast_fusion.2
  66.3 0.2 fusion
  66.5 1.9 %collective-permute-start.8 = (f32[38,6,1,128]{3,0,2,1:T(8,128)S(1)}, f32[38,6,1,128]{3,0,2,1:T(8,128)S(1)}, u32[]{:S(2)}, u32[]{:S(2)}) collective-permute-start(f32[38,6,1,128]{3,0,2,1:T(8,128)S(1)} %copy.267), channel_id=1, source_target_pairs={{0,2},{2,4},{4,6},{6,0},{1,3},{3,5},{5,7},{7,1},{8,10},{10,12},{12... | collective-permute-start | bytes 350216 | tf_op jit(solution)/shard_map/ppermute | solution.py:40
  68.4 0.5 collective-permute-start.9
  68.8 2.6 %collective-permute-done.8 = f32[38,6,1,128]{3,0,2,1:T(8,128)S(1)} collective-permute-done((f32[38,6,1,128]{3,0,2,1:T(8,128)S(1)}, f32[38,6,1,128]{3,0,2,1:T(8,128)S(1)}, u32[]{:S(2)}, u32[]{:S(2)}) %collective-permute-start.8) | collective-permute-done | bytes 116768 | tf_op jit(solution)/shard_map/ppermute | solution.py:40
  71.4 0.1 copy.268
  71.6 3.2 %collective-permute-done.9 = f32[38,6,1,128]{3,0,2,1:T(8,128)S(1)} collective-permute-done((f32[38,6,1,128]{3,0,2,1:T(8,128)S(1)}, f32[38,6,1,128]{3,0,2,1:T(8,128)S(1)}, u32[]{:S(2)}, u32[]{:S(2)}) %collective-permute-start.9) | collective-permute-done | bytes 116768 | tf_op jit(solution)/shard_map/ppermute | solution.py:42
  74.7 0.1 copy.270
  74.8 0.4 pad_maximum_fusion
  75.3 3.2 %fusion.105 = (f32[38,6,18,1]{3,2,0,1:T(8,128)}, f32[38,6,18,1]{3,2,0,1:T(8,128)}) fusion(f32[38,6,18,128]{3,2,0,1:T(8,128)S(1)} %pad_maximum_fusion), kind=kLoop, calls=%fused_computation.400 | loop fusion | bytes 65664 | tf_op jit(solution)/shard_map/slice | solution.py:36
  78.5 2.9 %copy.273 = f32[38,6,18,1]{0,2,3,1:T(8,128)S(1)} copy(f32[38,6,18,1]{3,2,0,1:T(8,128)} %get-tuple-element.55) | data formatting | bytes 32832 | tf_op jit(solution)/shard_map/slice | solution.py:37
  81.4 4.6 %collective-permute-start.10 = (f32[38,6,18,1]{0,2,3,1:T(8,128)S(1)}, f32[38,6,18,1]{0,2,3,1:T(8,128)S(1)}, u32[]{:S(2)}, u32[]{:S(2)}) collective-permute-start(f32[38,6,18,1]{0,2,3,1:T(8,128)S(1)} %copy.273), channel_id=1, source_target_pairs={{0,1},{1,0},{2,3},{3,2},{4,5},{5,4},{6,7},{7,6},{8,9},{9,8},{10,11... | collective-permute-start | bytes 49256 | tf_op jit(solution)/shard_map/ppermute | solution.py:40
  86.0 2.9 %copy.275 = f32[38,6,18,1]{0,2,3,1:T(8,128)S(1)} copy(f32[38,6,18,1]{3,2,0,1:T(8,128)} %get-tuple-element.54) | data formatting | bytes 32832 | tf_op jit(solution)/shard_map/slice | solution.py:36
  88.9 1.5 %collective-permute-start.11 = (f32[38,6,18,1]{0,2,3,1:T(8,128)S(1)}, f32[38,6,18,1]{0,2,3,1:T(8,128)S(1)}, u32[]{:S(2)}, u32[]{:S(2)}) collective-permute-start(f32[38,6,18,1]{0,2,3,1:T(8,128)S(1)} %copy.275), channel_id=1, source_target_pairs={{1,0},{0,1},{3,2},{2,3},{5,4},{4,5},{7,6},{6,7},{9,8},{8,9},{11,10... | collective-permute-start | bytes 49256 | tf_op jit(solution)/shard_map/ppermute | solution.py:42
  90.4 2.7 %copy.274 = f32[38,6,18,1]{3,2,0,1:T(8,128)} copy(f32[38,6,18,1]{0,2,3,1:T(8,128)S(1)} %collective-permute-done.10) | data formatting | bytes 32832 | tf_op jit(solution)/shard_map/ppermute | solution.py:40
  93.1 0.9 constant_dynamic-update-slice_fusion.91
  94.0 3.3 %collective-permute-done.11 = f32[38,6,18,1]{0,2,3,1:T(8,128)S(1)} collective-permute-done((f32[38,6,18,1]{0,2,3,1:T(8,128)S(1)}, f32[38,6,18,1]{0,2,3,1:T(8,128)S(1)}, u32[]{:S(2)}, u32[]{:S(2)}) %collective-permute-start.11) | collective-permute-done | bytes 16448 | tf_op jit(solution)/shard_map/ppermute | solution.py:42
  97.2 2.7 %copy.276 = f32[38,6,18,1]{3,2,0,1:T(8,128)} copy(f32[38,6,18,1]{0,2,3,1:T(8,128)S(1)} %collective-permute-done.11) | data formatting | bytes 32832 | tf_op jit(solution)/shard_map/ppermute | solution.py:42
  100.0 0.9 constant_dynamic-update-slice_fusion.90
  100.9 1.7 %copy-done.1 = f32[38,6,18,1]{3,2,0,1:T(8,128)S(1)} copy-done((f32[38,6,18,1]{3,2,0,1:T(8,128)S(1)}, f32[38,6,18,1]{3,2,0,1:T(8,128)}, u32[]{:S(2)}) %copy-start.1) | copy-done | bytes 16440
  102.6 0.1 constant_dynamic-update-slice_fusion.86
  102.7 1.7 %copy-done = f32[38,6,18,1]{3,2,0,1:T(8,128)S(1)} copy-done((f32[38,6,18,1]{3,2,0,1:T(8,128)S(1)}, f32[38,6,18,1]{3,2,0,1:T(8,128)}, u32[]{:S(2)}) %copy-start) | copy-done | bytes 16440
  104.4 0.1 constant_dynamic-update-slice_fusion.85
  104.5 0.1 constant_dynamic-update-slice_fusion.82
  104.6 0.1 constant_dynamic-update-slice_fusion.81
  104.7 1.0 copy-done.4
  105.7 0.1 constant_dynamic-update-slice_fusion.80
  105.8 0.1 constant_dynamic-update-slice_fusion.79
  105.9 0.1 constant_dynamic-update-slice_fusion.72
  106.0 0.1 constant_dynamic-update-slice_fusion.71
  106.1 0.1 constant_dynamic-update-slice_fusion.78
  106.2 0.1 constant_dynamic-update-slice_fusion.67
  106.3 0.1 constant_dynamic-update-slice_fusion.66
  106.4 0.1 constant_dynamic-update-slice_fusion.77
  106.5 0.9 copy.280
  107.4 0.1 constant_dynamic-update-slice_fusion.63
  107.5 0.1 constant_dynamic-update-slice_fusion.62
  107.6 0.1 constant_dynamic-update-slice_fusion.61
  107.7 0.1 constant_dynamic-update-slice_fusion.60
  107.8 0.1 constant_dynamic-update-slice_fusion.59
  107.9 0.1 constant_dynamic-update-slice_fusion.58
  108.0 0.9 copy.279
  (102 shorter events, 1.3 us)
Async XLA Ops:
  0.6 37.3 %copy-start.3 = (f32[19,4,16,128]{3,2,1,0:T(8,128)S(1)}, f32[19,4,16,128]{3,2,1,0:T(8,128)}, u32[]{:S(2)}) copy-start(f32[19,4,16,128]{3,2,1,0:T(8,128)} %param.4) | copy-start | bytes 1867780
  0.6 37.3 %copy-start.2 = (f32[19,4,16,128]{3,2,1,0:T(8,128)S(1)}, f32[19,4,16,128]{3,2,1,0:T(8,128)}, u32[]{:S(2)}) copy-start(f32[19,4,16,128]{3,2,1,0:T(8,128)} %param.3) | copy-start | bytes 1867780
  1.9 11.4 %collective-permute-start.3 = (f32[4,1,128]{2,1,0:T(1,128)S(1)}, f32[4,1,128]{2,1,0:T(1,128)S(1)}, u32[]{:S(2)}, u32[]{:S(2)}) collective-permute-start(f32[4,1,128]{2,1,0:T(1,128)S(1)} %get-tuple-element.100), channel_id=1, source_target_pairs={{2,0},{4,2},{6,4},{0,6},{3,1},{5,3},{7,5},{1,7},{10,8},{12,10},{14... | collective-permute-start | bytes 6152 | tf_op jit(solution)/shard_map/ppermute | solution.py:42
  2.8 10.5 %collective-permute-start.2 = (f32[4,1,128]{2,1,0:T(1,128)S(1)}, f32[4,1,128]{2,1,0:T(1,128)S(1)}, u32[]{:S(2)}, u32[]{:S(2)}) collective-permute-start(f32[4,1,128]{2,1,0:T(1,128)S(1)} %get-tuple-element.101), channel_id=1, source_target_pairs={{0,2},{2,4},{4,6},{6,0},{1,3},{3,5},{5,7},{7,1},{8,10},{10,12},{12... | collective-permute-start | bytes 6152 | tf_op jit(solution)/shard_map/ppermute | solution.py:40
  5.2 19.3 %collective-permute-start.1 = (f32[1,1,16,128]{3,2,1,0:T(8,128)S(1)}, f32[1,1,16,128]{3,2,1,0:T(8,128)S(1)}, u32[]{:S(2)}, u32[]{:S(2)}) collective-permute-start(f32[1,1,16,128]{3,2,1,0:T(8,128)S(1)} %get-tuple-element.106), channel_id=1, source_target_pairs={{8,0},{16,8},{24,16},{32,24},{40,32},{48,40},{56,48},{64,56},{72,6... | collective-permute-start | bytes 24584 | tf_op jit(solution)/shard_map/ppermute | solution.py:42
  11.2 8.1 %collective-permute-start = (f32[1,1,16,128]{3,2,1,0:T(8,128)S(1)}, f32[1,1,16,128]{3,2,1,0:T(8,128)S(1)}, u32[]{:S(2)}, u32[]{:S(2)}) collective-permute-start(f32[1,1,16,128]{3,2,1,0:T(8,128)S(1)} %get-tuple-element.107), channel_id=1, source_target_pairs={{0,8},{8,16},{16,24},{24,32},{32,40},{40,48},{48,56},{56,64},{64,7... | collective-permute-start | bytes 24584 | tf_op jit(solution)/shard_map/ppermute | solution.py:40
  13.4 23.1 %collective-permute-start.5 = (f32[4,18,1]{2,1,0:T(8,128)S(1)}, f32[4,18,1]{2,1,0:T(8,128)S(1)}, u32[]{:S(2)}, u32[]{:S(2)}) collective-permute-start(f32[4,18,1]{2,1,0:T(8,128)S(1)} %get-tuple-element.98), channel_id=1, source_target_pairs={{1,0},{0,1},{3,2},{2,3},{5,4},{4,5},{7,6},{6,7},{9,8},{8,9},{11,10... | collective-permute-start | bytes 872 | tf_op jit(solution)/shard_map/ppermute | solution.py:42
  17.9 18.6 %collective-permute-start.4 = (f32[4,18,1]{2,1,0:T(8,128)S(1)}, f32[4,18,1]{2,1,0:T(8,128)S(1)}, u32[]{:S(2)}, u32[]{:S(2)}) collective-permute-start(f32[4,18,1]{2,1,0:T(8,128)S(1)} %get-tuple-element.99), channel_id=1, source_target_pairs={{0,1},{1,0},{2,3},{3,2},{4,5},{5,4},{6,7},{7,6},{8,9},{9,8},{10,11... | collective-permute-start | bytes 872 | tf_op jit(solution)/shard_map/ppermute | solution.py:40
  20.0 16.4 %all-to-all-start = ((f32[4,1,16,128]{3,2,1,0:T(8,128)}), f32[4,1,16,128]{3,2,1,0:T(8,128)S(1)}, u32[]{:S(2)}, u32[]{:S(2)}) async-start(f32[4,1,16,128]{3,2,1,0:T(8,128)} %stack.152), calls=%async_computation | async-start | bytes 65536 | tf_op jit(solution)/shard_map/all_to_all | solution.py:119
  38.6 14.7 %collective-permute-start.7 = (f32[10,1,16,128]{3,2,0,1:T(8,128)S(1)}, f32[10,1,16,128]{3,2,0,1:T(8,128)S(1)}, u32[]{:S(2)}, u32[]{:S(2)}) collective-permute-start(f32[10,1,16,128]{3,2,0,1:T(8,128)S(1)} %get-tuple-element.84), channel_id=1, source_target_pairs={{8,0},{16,8},{24,16},{32,24},{40,32},{48,40},{56,48},{64,56},{72,6... | collective-permute-start | bytes 245768 | tf_op jit(solution)/shard_map/ppermute | solution.py:42
  40.3 7.8 %collective-permute-start.6 = (f32[10,1,16,128]{3,2,0,1:T(8,128)S(1)}, f32[10,1,16,128]{3,2,0,1:T(8,128)S(1)}, u32[]{:S(2)}, u32[]{:S(2)}) collective-permute-start(f32[10,1,16,128]{3,2,0,1:T(8,128)S(1)} %get-tuple-element.85), channel_id=1, source_target_pairs={{0,8},{8,16},{16,24},{24,32},{32,40},{40,48},{48,56},{56,64},{64,7... | collective-permute-start | bytes 245768 | tf_op jit(solution)/shard_map/ppermute | solution.py:40
  48.9 17.2 %all-to-all-start.1 = ((f32[4,10,16,128]{3,2,1,0:T(8,128)}), f32[4,10,16,128]{3,2,1,0:T(8,128)S(1)}, u32[]{:S(2)}, u32[]{:S(2)}) async-start(f32[4,10,16,128]{3,2,1,0:T(8,128)} %stack.180), calls=%async_computation.1 | async-start | bytes 655360 | tf_op jit(solution)/shard_map/all_to_all | solution.py:119
  66.5 5.0 %collective-permute-start.8 = (f32[38,6,1,128]{3,0,2,1:T(8,128)S(1)}, f32[38,6,1,128]{3,0,2,1:T(8,128)S(1)}, u32[]{:S(2)}, u32[]{:S(2)}) collective-permute-start(f32[38,6,1,128]{3,0,2,1:T(8,128)S(1)} %copy.267), channel_id=1, source_target_pairs={{0,2},{2,4},{4,6},{6,0},{1,3},{3,5},{5,7},{7,1},{8,10},{10,12},{12... | collective-permute-start | bytes 350216 | tf_op jit(solution)/shard_map/ppermute | solution.py:40
  68.4 6.3 %collective-permute-start.9 = (f32[38,6,1,128]{3,0,2,1:T(8,128)S(1)}, f32[38,6,1,128]{3,0,2,1:T(8,128)S(1)}, u32[]{:S(2)}, u32[]{:S(2)}) collective-permute-start(f32[38,6,1,128]{3,0,2,1:T(8,128)S(1)} %copy.269), channel_id=1, source_target_pairs={{2,0},{4,2},{6,4},{0,6},{3,1},{5,3},{7,5},{1,7},{10,8},{12,10},{14... | collective-permute-start | bytes 350216 | tf_op jit(solution)/shard_map/ppermute | solution.py:42
  81.4 9.0 %collective-permute-start.10 = (f32[38,6,18,1]{0,2,3,1:T(8,128)S(1)}, f32[38,6,18,1]{0,2,3,1:T(8,128)S(1)}, u32[]{:S(2)}, u32[]{:S(2)}) collective-permute-start(f32[38,6,18,1]{0,2,3,1:T(8,128)S(1)} %copy.273), channel_id=1, source_target_pairs={{0,1},{1,0},{2,3},{3,2},{4,5},{5,4},{6,7},{7,6},{8,9},{9,8},{10,11... | collective-permute-start | bytes 49256 | tf_op jit(solution)/shard_map/ppermute | solution.py:40
  88.9 8.3 %collective-permute-start.11 = (f32[38,6,18,1]{0,2,3,1:T(8,128)S(1)}, f32[38,6,18,1]{0,2,3,1:T(8,128)S(1)}, u32[]{:S(2)}, u32[]{:S(2)}) collective-permute-start(f32[38,6,18,1]{0,2,3,1:T(8,128)S(1)} %copy.275), channel_id=1, source_target_pairs={{1,0},{0,1},{3,2},{2,3},{5,4},{4,5},{7,6},{6,7},{9,8},{8,9},{11,10... | collective-permute-start | bytes 49256 | tf_op jit(solution)/shard_map/ppermute | solution.py:42
  100.8 1.8 %copy-start.1 = (f32[38,6,18,1]{3,2,0,1:T(8,128)S(1)}, f32[38,6,18,1]{3,2,0,1:T(8,128)}, u32[]{:S(2)}) copy-start(f32[38,6,18,1]{3,2,0,1:T(8,128)} %copy.276) | copy-start | bytes 49252
  102.6 1.8 %copy-start = (f32[38,6,18,1]{3,2,0,1:T(8,128)S(1)}, f32[38,6,18,1]{3,2,0,1:T(8,128)}, u32[]{:S(2)}) copy-start(f32[38,6,18,1]{3,2,0,1:T(8,128)} %copy.274) | copy-start | bytes 49252
  104.6 1.1 copy-start.4
